TPU v7x, 32 devices: a whole 2x2x4 slice. The times are simulated.
32 devices in a mesh: table: 4 (over y, x), batch: 4 (over z), ctx: 2 (over core).
Axes of the slice: x: 2, y: 2, z: 4, core: 2. Of those that a mesh axis runs over, the one named last changes fastest.
Arguments:
- item_table: bfloat16 [65536, 256], P('table')
- context_table: bfloat16 [4096, 256], replicated
- user_table: bfloat16 [16384, 256], P(('table', 'batch')), may hold values from -3 to 3
- item_owner: int32 [1024, 64, 1], P(('table', 'batch', 'ctx')), may hold values from 0 to 3; in each aligned block of 2048 rows (0 to 2047, 2048 to 4095, ..., all dimensions but the last counted through in order) at most 1024 rows name the same one
- item_row: int32 [1024, 64], P(('table', 'batch', 'ctx')), may hold values from 0 to 16383
- context_id: int32 [1024, 64], P(('table', 'batch', 'ctx')), may hold values from 0 to 4095
- bucket: int32 [1024, 64], P(('table', 'batch', 'ctx')), may hold values from 0 to 3
- user_ids: int32 [1024], P(('table', 'batch', 'ctx')), may hold values from 0 to 16383, as said below
Outputs:
- updated_users: bfloat16 [16384, 256], P(('table', 'batch'))
Inputs may be any that keep to these rules, and one draw needn't show every extreme that they name: `item_owner`: among the 2048 slots of one device no table shard is named more than 1024 times. `bucket`: 0 marks an empty slot. `user_ids`: all ids are distinct. User u is owned by index u // 1024 of table+batch at row u % 1024. At most 2 of the users of one device share an owner, and on every device some owner has exactly 2.
All inputs are finite; a program needn't handle non-finite values.
Results may differ from a plain program's by a relative error of at most 0.001.
Values may be sent and summed in bfloat16 or wider, within the bound.
No kernel may reach another device: no remote copies, remote signals or barrier semaphores. Data moves between devices by JAX's collectives and lax.ppermute only.
A program may use at most 64 MiB of HBM per device.

v0:
```python
import jax
import jax.numpy as jnp
from jax import lax
from jax.sharding import PartitionSpec as P

CG_STEPS = 3
REG_LAMBDA = 0.1
CONF_SCALE = 2.0
EPSILON = 1e-06


def gram_of(table_rows):
    return lax.dot_general(
        table_rows, table_rows, (((0,), (0,)), ((), ())), preferred_element_type=jnp.float32
    )


def owner_slots(owners, groups, capacity):
    one_hot = (jnp.arange(groups, dtype=jnp.int32)[:, None] == owners[None, :]).astype(jnp.int32)
    earlier = jnp.cumsum(one_hot, axis=1) - one_hot
    position = jnp.sum(earlier * one_hot, axis=0)
    return owners * capacity + position


def place_integers(values, placing):
    upper = (values // 128).astype(jnp.bfloat16)
    lower = (values % 128).astype(jnp.bfloat16)
    stacked = jnp.stack([upper, lower], axis=0)
    placed = lax.dot_general(
        stacked, placing, (((1,), (0,)), ((), ())), preferred_element_type=jnp.float32
    )
    return placed[0].astype(jnp.int32) * 128 + placed[1].astype(jnp.int32)


def conjugate_solve(slot_rows, confidence, weights, gram_matrix):
    highest = lax.Precision.HIGHEST
    rank_width = slot_rows.shape[-1]
    right_side = jnp.einsum(
        "usk,us->uk", slot_rows, weights, precision=highest, preferred_element_type=jnp.float32
    ) * rank_width ** (-0.5)
    solution = jnp.zeros_like(right_side)
    residual = right_side
    direction = right_side
    norm_now = jnp.sum(residual * residual, axis=1, keepdims=True)
    for iteration in range(CG_STEPS):
        projected = jnp.einsum(
            "usk,uk->us",
            slot_rows,
            direction,
            precision=highest,
            preferred_element_type=jnp.float32,
        )
        image_vec = (
            jnp.dot(direction, gram_matrix, precision=highest)
            + REG_LAMBDA * direction
            + jnp.einsum(
                "us,usk->uk",
                confidence * projected,
                slot_rows,
                precision=highest,
                preferred_element_type=jnp.float32,
            )
            / rank_width
        )
        step_size = norm_now / (jnp.sum(direction * image_vec, axis=1, keepdims=True) + EPSILON)
        solution = solution + step_size * direction
        residual = residual - step_size * image_vec
        norm_next = jnp.sum(residual * residual, axis=1, keepdims=True)
        direction = residual + norm_next / (norm_now + EPSILON) * direction
        norm_now = norm_next
    return solution


def per_device(
    item_table, context_table, user_table, item_owner, item_row, context_id, bucket, user_ids
):
    n_table = lax.axis_size("table")
    n_batch = lax.axis_size("batch")
    item_gram = lax.psum(gram_of(item_table).astype(jnp.bfloat16), "table").astype(jnp.float32)
    context_gram = gram_of(context_table)
    pair_count = item_table.shape[0] * n_table * context_table.shape[0]
    gram_matrix = item_gram * context_gram / pair_count
    user_count, slot_count = bucket.shape
    rank_width = item_table.shape[1]
    flat_count = user_count * slot_count
    capacity = 2 * flat_count // n_table
    owners = item_owner.reshape(flat_count)
    target = owner_slots(owners, n_table, capacity)
    placing = (target[:, None] == jnp.arange(n_table * capacity, dtype=jnp.int32)[None, :]).astype(
        jnp.bfloat16
    )
    row_requests = place_integers(item_row.reshape(flat_count), placing).reshape(n_table, capacity)
    context_flat = context_id.reshape(flat_count)
    fetched = lax.all_to_all(
        item_table[lax.all_to_all(row_requests, "table", split_axis=0, concat_axis=0, tiled=True)],
        "table",
        split_axis=0,
        concat_axis=0,
        tiled=True,
    )
    picked = jnp.dot(
        placing, fetched.reshape(n_table * capacity, rank_width), preferred_element_type=jnp.float32
    )
    slot_rows = (picked * context_table[context_flat].astype(jnp.float32)).astype(jnp.bfloat16)
    slot_rows = slot_rows.reshape(user_count, slot_count, rank_width)
    confidence = CONF_SCALE * bucket.astype(jnp.float32)
    weights = jnp.where(bucket > 0, 1.0 + confidence, 0.0)
    solved = conjugate_solve(slot_rows, confidence, weights, gram_matrix).astype(jnp.bfloat16)
    user_rows = user_table.shape[0]
    owner_count = n_table * n_batch
    user_capacity = (user_count + owner_count - 1) // owner_count
    user_owner = user_ids // user_rows
    local_rows = user_ids % user_rows
    user_target = owner_slots(user_owner, owner_count, user_capacity)
    user_placing = (
        user_target[:, None] == jnp.arange(owner_count * user_capacity, dtype=jnp.int32)[None, :]
    ).astype(jnp.bfloat16)
    send_rows = lax.dot_general(
        user_placing, solved, (((0,), (0,)), ((), ())), preferred_element_type=jnp.float32
    ).astype(jnp.bfloat16)
    filled = jnp.sum(user_placing.astype(jnp.float32), axis=0)
    placed_ids = place_integers(local_rows, user_placing)
    send_ids = jnp.where(filled > 0.5, placed_ids, user_rows)
    got_rows, got_ids = (
        lax.all_to_all(send_rows, ("table", "batch"), split_axis=0, concat_axis=0, tiled=True),
        lax.all_to_all(send_ids, ("table", "batch"), split_axis=0, concat_axis=0, tiled=True),
    )
    all_rows, all_ids = (
        lax.all_gather(got_rows, "ctx", axis=0, tiled=True),
        lax.all_gather(got_ids, "ctx", axis=0, tiled=True),
    )
    hitting = (jnp.arange(user_rows, dtype=jnp.int32)[:, None] == all_ids[None, :]).astype(
        jnp.bfloat16
    )
    landed = jnp.dot(hitting, all_rows, preferred_element_type=jnp.float32).astype(jnp.bfloat16)
    covered = jnp.sum(hitting.astype(jnp.float32), axis=1, keepdims=True) > 0.5
    return jnp.where(covered, landed, user_table)


def solution(mesh):
    in_specs = (
        P("table", None),
        P(),
        P(("table", "batch"), None),
        P(("table", "batch", "ctx"), None, None),
        P(("table", "batch", "ctx"), None),
        P(("table", "batch", "ctx"), None),
        P(("table", "batch", "ctx"), None),
        P(("table", "batch", "ctx")),
    )
    out_specs = P(("table", "batch"), None)
    return jax.shard_map(
        per_device, mesh=mesh, in_specs=in_specs, out_specs=out_specs, check_vma=False
    )
```

profile of v0, /device:TPU:0, one launch (start us, length us, event | category | flops | bytes accessed | tf_op | source)
XLA Modules:
  0.0 154.9 jit_solution(15914122811694390057)
XLA Ops:
  6.5 0.5 broadcast.313
  7.1 1.5 fusion.54
  8.7 1.1 reduce-window.6
  9.8 0.2 slice_reduce_fusion
  10.0 0.2 reduce-window.9
  10.4 0.8 reshape.350
  11.3 6.0 %fusion.1 = f32[2,4096]{1,0:T(2,128)S(1)} fusion(s32[2048]{0:T(1024)S(1)} %bitcast_add_fusion, bf16[1,2048]{1,0:T(2,128)(2,1)S(1)} %fusion.39, bf16[1,2048]{1,0:T(2,128)(2,1)S(1)} %get-tuple-element.16), kind=kOutput, calls=%fused_computation.4 | convolution fusion | flops 41959424 | bytes 49152 | tf_op jit(solution)/shard_map/dot_general | solution.py:29
  17.3 0.6 fusion.28
  17.9 5.2 %all-to-all-start.1 = ((s32[4,1,1024]{2,1,0:T(1,128)}), s32[4,1,1024]{2,1,0:T(1,128)S(1)}, u32[]{:S(2)}, u32[]{:S(2)}) async-start(s32[4,1,1024]{2,1,0:T(1,128)} %bitcast.5), calls=%async_computation.1 | async-start | bytes 32768 | tf_op jit(solution)/shard_map/all_to_all | solution.py:95
  23.1 0.2 reduce_window_sum.24
  23.3 0.1 convert_reduce_fusion.1
  23.4 0.2 fusion.34
  23.8 0.1 gt.35
  23.8 0.6 broadcast_select_fusion
  24.5 3.3 %all-to-all-done.1 = s32[4,1,1024]{2,1,0:T(1,128)S(1)} async-done(((s32[4,1,1024]{2,1,0:T(1,128)}), s32[4,1,1024]{2,1,0:T(1,128)S(1)}, u32[]{:S(2)}, u32[]{:S(2)}) %all-to-all-start.1) | async-done | bytes 16416 | tf_op jit(solution)/shard_map/all_to_all | solution.py:95
  27.8 5.0 %all-to-all-start = ((s32[16,2,1]{1,2,0:T(1,128)}), s32[16,2,1]{1,2,0:T(1,128)S(1)}, u32[]{:S(2)}, u32[]{:S(2)}) async-start(s32[16,2,1]{1,2,0:T(1,128)} %bitcast.2), calls=%async_computation | async-start | bytes 16384 | tf_op jit(solution)/shard_map/all_to_all | solution.py:126
  32.9 20.3 %gather_fusion = bf16[4096,256]{1,0:T(8,128)(2,1)} fusion(bf16[16384,256]{1,0:T(8,128)(2,1)} %param.8, s32[4096]{0:T(1024)S(1)} %broadcast_clamp_fusion), kind=kCustom, calls=%fused_computation | custom fusion | bytes 4210688 | tf_op jit(solution)/shard_map/gather | solution.py:95
  53.1 4.4 %all-to-all-start.2 = ((bf16[4,1024,256]{2,1,0:T(8,128)(2,1)}), bf16[4,1024,256]{2,1,0:T(8,128)(2,1)}, u32[]{:S(2)}, u32[]{:S(2)}) async-start(bf16[4,1024,256]{2,1,0:T(8,128)(2,1)} %bitcast.110), calls=%async_computation.2 | async-start | bytes 4194304 | tf_op jit(solution)/shard_map/all_to_all | solution.py:94
  57.6 0.2 all-reduce.3.cloned.1.call-start
  57.9 8.8 %convolution_convert_fusion.1 = bf16[256,256]{1,0:T(8,128)(2,1)} fusion(bf16[16384,256]{1,0:T(8,128)(2,1)} %param.8), kind=kOutput, calls=%fused_computation.13 | convolution fusion | flops 2147549184 | bytes 8519680 | tf_op jit(solution)/shard_map/dot_general | solution.py:13
  66.9 7.5 %gather_fusion.1 = bf16[2048,256]{1,0:T(8,128)(2,1)S(1)} fusion(bf16[4096,256]{1,0:T(8,128)(2,1)S(1)} %copy-done, s32[2048]{0:T(1024)S(1)} %broadcast_clamp_fusion.1), kind=kCustom, calls=%fused_computation.1 | custom fusion | bytes 2105344 | tf_op jit(solution)/shard_map/gather | solution.py:104
  74.4 0.6 dynamic-slice
  75.6 0.6 reduce.18
  76.2 0.1 reshape.371
  76.3 0.2 dynamic-update-slice
  76.6 1.8 %all-reduce = s32[64]{0:T(128)S(1)} all-reduce(s32[64]{0:T(128)S(1)} %dynamic-update-slice), channel_id=1, replica_groups=mesh['table'=4,'batch'=4,'ctx'=2] {'ctx'}, use_global_device_ids=true, to_apply=%add | all-reduce | flops 64 | bytes 512
  78.4 0.1 convert_reduce_fusion
  78.5 36.9 %all-reduce.3.cloned.1.call-done = bf16[256,256]{1,0:T(8,128)(2,1)} async-done(((bf16[256,256]{1,0:T(8,128)(2,1)}), bf16[256,256]{1,0:T(8,128)(2,1)}) %all-reduce.3.cloned.1.call-update) | async-done | bytes 131088 | tf_op jit(solution)/shard_map/psum | solution.py:79
  115.4 1.6 %fusion.7 = f32[256,256]{1,0:T(8,128)S(1)} fusion(bf16[4096,256]{1,0:T(8,128)(2,1)S(1)} %copy-done, bf16[256,256]{1,0:T(8,128)(2,1)} %all-reduce.3.cloned.1.call-done), kind=kOutput, calls=%fused_computation.12 | convolution fusion | flops 537067520 | bytes 2490368 | tf_op jit(solution)/shard_map/dot_general | solution.py:13
  117.1 7.4 %fusion.5 = bf16[2048,256]{1,0:T(8,128)(2,1)S(1)} fusion(bf16[4096,256]{1,0:T(8,128)(2,1)} %bitcast.9, s32[2048]{0:T(1024)S(1)} %bitcast_add_fusion, bf16[2048,256]{1,0:T(8,128)(2,1)S(1)} %gather_fusion.1), kind=kOutput, calls=%fused_computation.8 | convolution fusion | flops 4304928768 | bytes 4202496 | tf_op jit(solution)/shard_map/dot_general | solution.py:101
  124.5 0.5 fusion.55
  125.0 0.9 fusion.23
  126.0 0.5 fusion.56
  126.5 0.3 multiply_reduce_fusion.3
  126.9 0.2 multiply_reduce_fusion.2
  127.1 0.9 fusion.21
  128.1 0.5 fusion.57
  128.6 0.3 multiply_reduce_fusion.1
  129.0 0.2 multiply_reduce_fusion
  129.3 0.9 fusion.19
  130.2 0.5 fusion.58
  130.7 0.3 fusion.12
  131.1 0.3 convolution_convert_fusion.2
  131.4 0.6 all_to_all.28
  132.0 5.6 %all-to-all-start.3 = ((bf16[16,2,256]{2,1,0:T(2,128)(2,1)}), bf16[16,2,256]{2,1,0:T(2,128)(2,1)S(1)}, u32[]{:S(2)}, u32[]{:S(2)}) async-start(bf16[16,2,256]{2,1,0:T(2,128)(2,1)} %all_to_all.28), calls=%async_computation.3 | async-start | bytes 32768 | tf_op jit(solution)/shard_map/all_to_all | solution.py:125
  137.6 7.3 %all-to-all-done.3 = bf16[16,2,256]{2,1,0:T(2,128)(2,1)S(1)} async-done(((bf16[16,2,256]{2,1,0:T(2,128)(2,1)}), bf16[16,2,256]{2,1,0:T(2,128)(2,1)S(1)}, u32[]{:S(2)}, u32[]{:S(2)}) %all-to-all-start.3) | async-done | bytes 16416 | tf_op jit(solution)/shard_map/all_to_all | solution.py:125
  144.9 1.8 %all_gather.7 = bf16[64,256]{1,0:T(8,128)(2,1)S(1)} all-gather(bf16[32,256]{1,0:T(8,128)(2,1)S(1)} %all_to_all.30), channel_id=1, replica_groups=mesh['table'=4,'batch'=4,'ctx'=2] {'ctx'}, dimensions={0}, use_global_device_ids=true | all-gather | bytes 49152 | tf_op jit(solution)/shard_map/all_gather | solution.py:129
  146.8 1.3 fusion.6
  (51 shorter events, 0.9 us)
Async XLA Ops:
  6.5 60.3 %copy-start = (bf16[4096,256]{1,0:T(8,128)(2,1)S(1)}, bf16[4096,256]{1,0:T(8,128)(2,1)}, u32[]{:S(2)}) copy-start(bf16[4096,256]{1,0:T(8,128)(2,1)} %param.9) | copy-start | bytes 6291460
  11.3 11.8 %copy-start.4 = (s32[32]{0:T(128)S(1)}, s32[32]{0:T(128)}, u32[]{:S(2)}) copy-start(s32[32]{0:T(128)} %param.15) | copy-start | bytes 388
  17.9 9.9 %all-to-all-start.1 = ((s32[4,1,1024]{2,1,0:T(1,128)}), s32[4,1,1024]{2,1,0:T(1,128)S(1)}, u32[]{:S(2)}, u32[]{:S(2)}) async-start(s32[4,1,1024]{2,1,0:T(1,128)} %bitcast.5), calls=%async_computation.1 | async-start | bytes 32768 | tf_op jit(solution)/shard_map/all_to_all | solution.py:95
  27.8 25.4 %all-to-all-start = ((s32[16,2,1]{1,2,0:T(1,128)}), s32[16,2,1]{1,2,0:T(1,128)S(1)}, u32[]{:S(2)}, u32[]{:S(2)}) async-start(s32[16,2,1]{1,2,0:T(1,128)} %bitcast.2), calls=%async_computation | async-start | bytes 16384 | tf_op jit(solution)/shard_map/all_to_all | solution.py:126
  53.1 63.9 %all-to-all-start.2 = ((bf16[4,1024,256]{2,1,0:T(8,128)(2,1)}), bf16[4,1024,256]{2,1,0:T(8,128)(2,1)}, u32[]{:S(2)}, u32[]{:S(2)}) async-start(bf16[4,1024,256]{2,1,0:T(8,128)(2,1)} %bitcast.110), calls=%async_computation.2 | async-start | bytes 4194304 | tf_op jit(solution)/shard_map/all_to_all | solution.py:94
  57.6 9.1 %copy-start.3 = (s32[32,64]{1,0:T(8,128)S(1)}, s32[32,64]{1,0:T(8,128)}, u32[]{:S(2)}) copy-start(s32[32,64]{1,0:T(8,128)} %param.13) | copy-start | bytes 24580
  57.6 9.2 %copy-start.2 = (s32[32,64]{1,0:T(8,128)S(1)}, s32[32,64]{1,0:T(8,128)}, u32[]{:S(2)}) copy-start(s32[32,64]{1,0:T(8,128)} %param.14) | copy-start | bytes 24580
  57.6 57.8 %all-reduce.3.cloned.1.call-start = ((), (), s32[]{:S(2)}) async-start(), calls=%async_computation.4 | async-start | bytes 262144 | tf_op jit(solution)/shard_map/psum | solution.py:79
  66.8 7.5 %copy-start.5 = (u32[32]{0:T(128)S(1)}, u32[32]{0:T(128)}, u32[]{:S(2)}) copy-start(u32[32]{0:T(128)} %constant.113) | copy-start | bytes 388
  128.1 18.7 %copy-start.1 = (bf16[1024,256]{1,0:T(8,128)(2,1)S(1)}, bf16[1024,256]{1,0:T(8,128)(2,1)}, u32[]{:S(2)}) copy-start(bf16[1024,256]{1,0:T(8,128)(2,1)} %param.10) | copy-start | bytes 1572868
  132.0 12.9 %all-to-all-start.3 = ((bf16[16,2,256]{2,1,0:T(2,128)(2,1)}), bf16[16,2,256]{2,1,0:T(2,128)(2,1)S(1)}, u32[]{:S(2)}, u32[]{:S(2)}) async-start(bf16[16,2,256]{2,1,0:T(2,128)(2,1)} %all_to_all.28), calls=%async_computation.3 | async-start | bytes 32768 | tf_op jit(solution)/shard_map/all_to_all | solution.py:125
Sparse Core Ops, SparseCore 0:
  66.8 48.5 all-reduce.2
where the time goes:
time: 155 us
  waiting for transfers between devices  47.6 us (31%)
  matrix products  31.5 us (20%)
  local copies, waits for them, and re-layouts  31.4 us (20%)
  starting transfers between devices  20.5 us (13%)
  between operations  14.3 us (9%)
  other arithmetic  6.01 us (4%)
  blocking collectives  3.64 us (2%)
    psum x1, waiting for transfers between devices, per_device(): lax.psum(gram_of(item_table).astype(jnp.bfloat16), 'table')  36.9 us
    gather x1, local copies, waits for them, and re-layouts, per_device(): item_table[lax.all_to_all(row_requests, 'table', split_axis=0, concat_axi...  20.3 us
    dot_general x2, matrix products, gram_of(): lax.dot_general(table_rows, table_rows, (((0,), (0,)), ((), ())), preferr...  10.5 us
    gather x1, local copies, waits for them, and re-layouts, per_device(): context_table[context_flat].astype(jnp.float32)  7.5 us
    dot_general x1, matrix products, per_device(): jnp.dot(placing, fetched.reshape(n_table * capacity, rank_width), preferr...  7.39 us
    all_to_all x1, waiting for transfers between devices, per_device(): lax.all_to_all(send_rows, ('table', 'batch'), split_axis=0, concat_axis=0...  7.3 us
    dot_general x2, matrix products, place_integers(): lax.dot_general(stacked, placing, (((1,), (0,)), ((), ())), preferred_ele...  6.17 us
    all_to_all x1, starting transfers between devices, per_device(): lax.all_to_all(send_rows, ('table', 'batch'), split_axis=0, concat_axis=0...  5.61 us
  transfers between devices with their start and end apart: 5, of which 3 were waited for; matrix products, arithmetic and copies ran while one was open for 27% of the time, Pallas kernels for 0%

commit v1 on v0

--- a/solution.py
+++ b/solution.py
@@ -7,6 +7,28 @@
 REG_LAMBDA = 0.1
 CONF_SCALE = 2.0
 EPSILON = 1e-06
+
+
+def cut_along(shard, dim, devices):
+    before, after = (shard.shape[:dim], shard.shape[dim + 1 :])
+    return jnp.moveaxis(shard.reshape(*before, devices, -1, *after), dim, 0)
+
+
+def laid_out(pieces, dim):
+    shape = list(pieces.shape[1:])
+    shape[dim] *= pieces.shape[0]
+    return jnp.moveaxis(pieces, 0, dim).reshape(shape)
+
+
+def exchange_in_pairs(x, axis, split_dim, concat_dim):
+    devices, index = (lax.axis_size(axis), lax.axis_index(axis))
+    parts = cut_along(x, split_dim, devices)
+    outs = [parts[index]]
+    for step in range(1, devices):
+        sent = parts[index ^ step]
+        outs.append(lax.ppermute(sent, axis, [(i, i ^ step) for i in range(devices)]))
+    parts = jnp.stack(outs)[index ^ jnp.arange(devices)]
+    return laid_out(parts, concat_dim)
 
 
 def gram_of(table_rows):
@@ -122,7 +144,7 @@
     placed_ids = place_integers(local_rows, user_placing)
     send_ids = jnp.where(filled > 0.5, placed_ids, user_rows)
     got_rows, got_ids = (
-        lax.all_to_all(send_rows, ("table", "batch"), split_axis=0, concat_axis=0, tiled=True),
+        exchange_in_pairs(send_rows, ("table", "batch"), 0, 0),
         lax.all_to_all(send_ids, ("table", "batch"), split_axis=0, concat_axis=0, tiled=True),
     )
     all_rows, all_ids = (

time: 155 us -> 149 us (0.961)
  waiting for transfers between devices: 47.6 us -> 17.1 us
  starting transfers between devices: 20.5 us -> 44.3 us
    psum x1, waiting for transfers between devices: 36.9 us -> 2.61 us  [per_device(): lax.psum(gram_of(item_table).astype(jnp.bfloat16), 'table')]
    ppermute x0 -> x15, starting transfers between devices: none -> 27 us  [exchange_in_pairs(): lax.ppermute(sent, axis, [(i, i ^ step) for i in range(devices)])]
    all_to_all x1, waiting for transfers between devices: 0.01 us -> 8.82 us  [per_device(): lax.all_to_all(item_table[lax.all_to_all(row_requests, 'table', split_axi...]
    all_to_all x1 -> x0, waiting for transfers between devices: 7.3 us -> none  [per_device(): lax.all_to_all(send_rows, ('table', 'batch'), split_axis=0, concat_axis=0...]
    ppermute x0 -> x15, waiting for transfers between devices: none -> 5.69 us  [exchange_in_pairs(): lax.ppermute(sent, axis, [(i, i ^ step) for i in range(devices)])]
    all_to_all x1 -> x0, starting transfers between devices: 5.61 us -> none  [per_device(): lax.all_to_all(send_rows, ('table', 'batch'), split_axis=0, concat_axis=0...]
    all_to_all x1, waiting for transfers between devices: 3.32 us -> 0.01 us  [per_device(): lax.all_to_all(row_requests, 'table', split_axis=0, concat_axis=0, tiled=...]
    all_to_all x1, starting transfers between devices: 5.03 us -> 7.33 us  [per_device(): lax.all_to_all(send_ids, ('table', 'batch'), split_axis=0, concat_axis=0,...]
  transfers between devices with their start and end apart: 5 -> 19, of which waited for: 3 -> 4; matrix products, arithmetic and copies ran while one was open for 27% -> 28% of each run, Pallas kernels for 0% -> 0%
where the time goes in v1:
time: 149 us
  starting transfers between devices  44.3 us (30%)
  local copies, waits for them, and re-layouts  31.6 us (21%)
  matrix products  31.5 us (21%)
  waiting for transfers between devices  17.1 us (11%)
  between operations  14.5 us (10%)
  other arithmetic  6.01 us (4%)
  blocking collectives  3.64 us (2%)
    ppermute x15, starting transfers between devices, exchange_in_pairs(): lax.ppermute(sent, axis, [(i, i ^ step) for i in range(devices)])  27 us
    gather x1, local copies, waits for them, and re-layouts, per_device(): item_table[lax.all_to_all(row_requests, 'table', split_axis=0, concat_axi...  20.3 us
    dot_general x2, matrix products, gram_of(): lax.dot_general(table_rows, table_rows, (((0,), (0,)), ((), ())), preferr...  10.5 us
    all_to_all x1, waiting for transfers between devices, per_device(): lax.all_to_all(item_table[lax.all_to_all(row_requests, 'table', split_axi...  8.82 us
    gather x1, local copies, waits for them, and re-layouts, per_device(): context_table[context_flat].astype(jnp.float32)  7.5 us
    dot_general x1, matrix products, per_device(): jnp.dot(placing, fetched.reshape(n_table * capacity, rank_width), preferr...  7.37 us
    all_to_all x1, starting transfers between devices, per_device(): lax.all_to_all(send_ids, ('table', 'batch'), split_axis=0, concat_axis=0,...  7.33 us
    dot_general x2, matrix products, place_integers(): lax.dot_general(stacked, placing, (((1,), (0,)), ((), ())), preferred_ele...  6.17 us
  transfers between devices with their start and end apart: 19, of which 4 were waited for; matrix products, arithmetic and copies ran while one was open for 28% of the time, Pallas kernels for 0%

profile of v1, /device:TPU:0, one launch (start us, length us, event | category | flops | bytes accessed | tf_op | source)
XLA Modules:
  0.0 148.7 jit_solution(2330210196168612500)
XLA Ops:
  6.5 0.5 broadcast.357
  7.1 1.5 %fusion.70 = (s32[32,64]{1,0:T(8,128)S(1)}, s32[32,64]{1,0:T(8,128)S(1)}) fusion(s32[32,64,1]{1,2,0:T(1,128)} %param.11, s32[]{:T(128)} %broadcast.357), kind=kLoop, calls=%fused_computation.176 | loop fusion | flops 2048 | bytes 24580 | tf_op args[3]
  8.7 1.1 reduce-window.6
  10.4 0.8 reshape.370
  11.3 6.0 %fusion.1 = f32[2,4096]{1,0:T(2,128)S(1)} fusion(s32[2048]{0:T(1024)S(1)} %bitcast_add_fusion, bf16[1,2048]{1,0:T(2,128)(2,1)S(1)} %fusion.39, bf16[1,2048]{1,0:T(2,128)(2,1)S(1)} %get-tuple-element.16), kind=kOutput, calls=%fused_computation.5 | convolution fusion | flops 41959424 | bytes 49152 | tf_op jit(solution)/shard_map/dot_general | solution.py:51
  17.2 0.6 fusion.28
  17.9 5.2 %all-to-all-start.1 = ((s32[4,1,1024]{2,1,0:T(1,128)}), s32[4,1,1024]{2,1,0:T(1,128)S(1)}, u32[]{:S(2)}, u32[]{:S(2)}) async-start(s32[4,1,1024]{2,1,0:T(1,128)} %bitcast.5), calls=%async_computation.1 | async-start | bytes 32768 | tf_op jit(solution)/shard_map/all_to_all | solution.py:117
  23.1 8.8 %convolution_convert_fusion.1 = bf16[256,256]{1,0:T(8,128)(2,1)} fusion(bf16[16384,256]{1,0:T(8,128)(2,1)} %param.8), kind=kOutput, calls=%fused_computation.14 | convolution fusion | flops 2147549184 | bytes 8519680 | tf_op jit(solution)/shard_map/dot_general | solution.py:35
  32.7 0.6 broadcast_select_fusion
  33.4 7.3 %all-to-all-start = ((s32[16,2,1]{1,2,0:T(1,128)}), s32[16,2,1]{1,2,0:T(1,128)S(1)}, u32[]{:S(2)}, u32[]{:S(2)}) async-start(s32[16,2,1]{1,2,0:T(1,128)} %bitcast.2), calls=%async_computation | async-start | bytes 16384 | tf_op jit(solution)/shard_map/all_to_all | solution.py:148
  40.8 20.3 %gather_fusion = bf16[4096,256]{1,0:T(8,128)(2,1)} fusion(bf16[16384,256]{1,0:T(8,128)(2,1)} %param.8, s32[4096]{0:T(1024)S(1)} %broadcast_clamp_fusion), kind=kCustom, calls=%fused_computation | custom fusion | bytes 4210688 | tf_op jit(solution)/shard_map/gather | solution.py:117
  61.1 4.8 %all-to-all-start.2 = ((bf16[4,1024,256]{2,1,0:T(8,128)(2,1)}), bf16[4,1024,256]{2,1,0:T(8,128)(2,1)}, u32[]{:S(2)}, u32[]{:S(2)}) async-start(bf16[4,1024,256]{2,1,0:T(8,128)(2,1)} %bitcast.172), calls=%async_computation.2 | async-start | bytes 4194304 | tf_op jit(solution)/shard_map/all_to_all | solution.py:116
  66.1 7.5 %gather_fusion.1 = bf16[2048,256]{1,0:T(8,128)(2,1)S(1)} fusion(bf16[4096,256]{1,0:T(8,128)(2,1)S(1)} %copy-done, s32[2048]{0:T(1024)S(1)} %broadcast_clamp_fusion.1), kind=kCustom, calls=%fused_computation.1 | custom fusion | bytes 2105344 | tf_op jit(solution)/shard_map/gather | solution.py:126
  73.7 0.6 dynamic-slice
  74.9 0.6 reduce.18
  75.9 1.8 %all-reduce = s32[64]{0:T(128)S(1)} all-reduce(s32[64]{0:T(128)S(1)} %dynamic-update-slice), channel_id=1, replica_groups=mesh['table'=4,'batch'=4,'ctx'=2] {'ctx'}, use_global_device_ids=true, to_apply=%add | all-reduce | flops 64 | bytes 512
  77.8 2.6 %all-reduce.3.cloned.1.call-done = bf16[256,256]{1,0:T(8,128)(2,1)} async-done(((bf16[256,256]{1,0:T(8,128)(2,1)}), bf16[256,256]{1,0:T(8,128)(2,1)}) %all-reduce.3.cloned.1.call-update) | async-done | bytes 131088 | tf_op jit(solution)/shard_map/psum | solution.py:101
  80.4 1.6 %fusion.7 = f32[256,256]{1,0:T(8,128)S(1)} fusion(bf16[4096,256]{1,0:T(8,128)(2,1)S(1)} %copy-done, bf16[256,256]{1,0:T(8,128)(2,1)} %all-reduce.3.cloned.1.call-done), kind=kOutput, calls=%fused_computation.13 | convolution fusion | flops 537067520 | bytes 2490368 | tf_op jit(solution)/shard_map/dot_general | solution.py:35
  82.1 8.8 %all-to-all-done.2 = bf16[4,1024,256]{2,1,0:T(8,128)(2,1)} async-done(((bf16[4,1024,256]{2,1,0:T(8,128)(2,1)}), bf16[4,1024,256]{2,1,0:T(8,128)(2,1)}, u32[]{:S(2)}, u32[]{:S(2)}) %all-to-all-start.2) | async-done | bytes 2097184 | tf_op jit(solution)/shard_map/all_to_all | solution.py:116
  90.9 7.4 %fusion.5 = bf16[2048,256]{1,0:T(8,128)(2,1)S(1)} fusion(bf16[4096,256]{1,0:T(8,128)(2,1)} %bitcast.9, s32[2048]{0:T(1024)S(1)} %bitcast_add_fusion, bf16[2048,256]{1,0:T(8,128)(2,1)S(1)} %gather_fusion.1), kind=kOutput, calls=%fused_computation.9 | convolution fusion | flops 4304928768 | bytes 4202496 | tf_op jit(solution)/shard_map/dot_general | solution.py:123
  98.3 0.5 fusion.71
  98.8 0.9 fusion.23
  99.7 0.5 fusion.72
  100.3 0.3 multiply_reduce_fusion.3
  100.9 0.9 fusion.21
  101.9 0.5 fusion.73
  102.4 0.3 multiply_reduce_fusion.1
  103.0 0.9 fusion.19
  104.0 0.5 fusion.74
  104.5 0.3 fusion.12
  105.3 1.6 %collective-permute-start = (bf16[2,256]{1,0:T(2,128)(2,1)S(1)}, bf16[2,256]{1,0:T(2,128)(2,1)S(1)}, u32[]{:S(2)}, u32[]{:S(2)}) collective-permute-start(bf16[2,256]{1,0:T(2,128)(2,1)S(1)} %get-tuple-element.32), channel_id=1, source_target_pairs={{0,2},{2,0},{4,6},{6,4},{8,10},{10,8},{12,14},{14,12},{16,18},{18,... | collective-permute-start | bytes 3080 | tf_op jit(solution)/shard_map/ppermute | solution.py:29
  106.9 2.4 %collective-permute-start.1 = (bf16[2,256]{1,0:T(2,128)(2,1)S(1)}, bf16[2,256]{1,0:T(2,128)(2,1)S(1)}, u32[]{:S(2)}, u32[]{:S(2)}) collective-permute-start(bf16[2,256]{1,0:T(2,128)(2,1)S(1)} %get-tuple-element.31), channel_id=1, source_target_pairs={{0,4},{2,6},{4,0},{6,2},{8,12},{10,14},{12,8},{14,10},{16,20},{18,... | collective-permute-start | bytes 3080 | tf_op jit(solution)/shard_map/ppermute | solution.py:29
  109.2 0.5 collective-permute-start.2
  109.7 1.4 collective-permute-start.3
  111.2 0.7 collective-permute-start.4
  111.8 4.1 %collective-permute-start.5 = (bf16[2,256]{1,0:T(2,128)(2,1)S(1)}, bf16[2,256]{1,0:T(2,128)(2,1)S(1)}, u32[]{:S(2)}, u32[]{:S(2)}) collective-permute-start(bf16[2,256]{1,0:T(2,128)(2,1)S(1)} %get-tuple-element.27), channel_id=1, source_target_pairs={{0,12},{2,14},{4,8},{6,10},{8,4},{10,6},{12,0},{14,2},{16,28},{18,... | collective-permute-start | bytes 3080 | tf_op jit(solution)/shard_map/ppermute | solution.py:29
  116.0 0.6 collective-permute-start.6
  116.6 1.5 %collective-permute-start.7 = (bf16[2,256]{1,0:T(2,128)(2,1)S(1)}, bf16[2,256]{1,0:T(2,128)(2,1)S(1)}, u32[]{:S(2)}, u32[]{:S(2)}) collective-permute-start(bf16[2,256]{1,0:T(2,128)(2,1)S(1)} %get-tuple-element.25), channel_id=1, source_target_pairs={{0,16},{2,18},{4,20},{6,22},{8,24},{10,26},{12,28},{14,30},{16,0},... | collective-permute-start | bytes 3080 | tf_op jit(solution)/shard_map/ppermute | solution.py:29
  118.2 4.8 %collective-permute-start.9 = (bf16[2,256]{1,0:T(2,128)(2,1)S(1)}, bf16[2,256]{1,0:T(2,128)(2,1)S(1)}, u32[]{:S(2)}, u32[]{:S(2)}) collective-permute-start(bf16[2,256]{1,0:T(2,128)(2,1)S(1)} %get-tuple-element.23), channel_id=1, source_target_pairs={{0,20},{2,22},{4,16},{6,18},{8,28},{10,30},{12,24},{14,26},{16,4},... | collective-permute-start | bytes 3080 | tf_op jit(solution)/shard_map/ppermute | solution.py:29
  123.0 0.5 collective-permute-start.10
  123.6 1.5 %collective-permute-start.11 = (bf16[2,256]{1,0:T(2,128)(2,1)S(1)}, bf16[2,256]{1,0:T(2,128)(2,1)S(1)}, u32[]{:S(2)}, u32[]{:S(2)}) collective-permute-start(bf16[2,256]{1,0:T(2,128)(2,1)S(1)} %get-tuple-element.21), channel_id=1, source_target_pairs={{0,24},{2,26},{4,28},{6,30},{8,16},{10,18},{12,20},{14,22},{16,8},... | collective-permute-start | bytes 3080 | tf_op jit(solution)/shard_map/ppermute | solution.py:29
  125.1 1.1 collective-permute-start.12
  126.2 4.7 %collective-permute-start.13 = (bf16[2,256]{1,0:T(2,128)(2,1)S(1)}, bf16[2,256]{1,0:T(2,128)(2,1)S(1)}, u32[]{:S(2)}, u32[]{:S(2)}) collective-permute-start(bf16[2,256]{1,0:T(2,128)(2,1)S(1)} %get-tuple-element.19), channel_id=1, source_target_pairs={{0,28},{2,30},{4,24},{6,26},{8,20},{10,22},{12,16},{14,18},{16,12}... | collective-permute-start | bytes 3080 | tf_op jit(solution)/shard_map/ppermute | solution.py:29
  130.9 1.5 collective-permute-start.14
  132.5 5.6 %collective-permute-done.14 = bf16[2,256]{1,0:T(2,128)(2,1)S(1)} collective-permute-done((bf16[2,256]{1,0:T(2,128)(2,1)S(1)}, bf16[2,256]{1,0:T(2,128)(2,1)S(1)}, u32[]{:S(2)}, u32[]{:S(2)}) %collective-permute-start.14) | collective-permute-done | bytes 1056 | tf_op jit(solution)/shard_map/ppermute | solution.py:29
  138.1 0.6 gather_fusion.2
  138.7 1.8 %all_gather.7 = bf16[64,256]{1,0:T(8,128)(2,1)S(1)} all-gather(bf16[32,256]{1,0:T(8,128)(2,1)S(1)} %reshape.375), channel_id=1, replica_groups=mesh['table'=4,'batch'=4,'ctx'=2] {'ctx'}, dimensions={0}, use_global_device_ids=true | all-gather | bytes 49152 | tf_op jit(solution)/shard_map/all_gather | solution.py:151
  140.6 1.3 fusion.6
  (98 shorter events, 3.5 us)
Async XLA Ops:
  6.5 59.5 %copy-start = (bf16[4096,256]{1,0:T(8,128)(2,1)S(1)}, bf16[4096,256]{1,0:T(8,128)(2,1)}, u32[]{:S(2)}) copy-start(bf16[4096,256]{1,0:T(8,128)(2,1)} %param.9) | copy-start | bytes 6291460
  17.9 15.5 %all-to-all-start.1 = ((s32[4,1,1024]{2,1,0:T(1,128)}), s32[4,1,1024]{2,1,0:T(1,128)S(1)}, u32[]{:S(2)}, u32[]{:S(2)}) async-start(s32[4,1,1024]{2,1,0:T(1,128)} %bitcast.5), calls=%async_computation.1 | async-start | bytes 32768 | tf_op jit(solution)/shard_map/all_to_all | solution.py:117
  23.0 8.9 %copy-start.4 = (s32[32]{0:T(128)S(1)}, s32[32]{0:T(128)}, u32[]{:S(2)}) copy-start(s32[32]{0:T(128)} %param.15) | copy-start | bytes 388
  23.0 10.3 %copy-start.3 = (s32[32,64]{1,0:T(8,128)S(1)}, s32[32,64]{1,0:T(8,128)}, u32[]{:S(2)}) copy-start(s32[32,64]{1,0:T(8,128)} %param.13) | copy-start | bytes 24580
  23.0 57.4 %all-reduce.3.cloned.1.call-start = ((), (), s32[]{:S(2)}) async-start(), calls=%async_computation.3 | async-start | bytes 262144 | tf_op jit(solution)/shard_map/psum | solution.py:101
  33.4 27.7 %all-to-all-start = ((s32[16,2,1]{1,2,0:T(1,128)}), s32[16,2,1]{1,2,0:T(1,128)S(1)}, u32[]{:S(2)}, u32[]{:S(2)}) async-start(s32[16,2,1]{1,2,0:T(1,128)} %bitcast.2), calls=%async_computation | async-start | bytes 16384 | tf_op jit(solution)/shard_map/all_to_all | solution.py:148
  61.1 4.8 %copy-start.2 = (s32[32,64]{1,0:T(8,128)S(1)}, s32[32,64]{1,0:T(8,128)}, u32[]{:S(2)}) copy-start(s32[32,64]{1,0:T(8,128)} %param.14) | copy-start | bytes 24580
  61.1 29.8 %all-to-all-start.2 = ((bf16[4,1024,256]{2,1,0:T(8,128)(2,1)}), bf16[4,1024,256]{2,1,0:T(8,128)(2,1)}, u32[]{:S(2)}, u32[]{:S(2)}) async-start(bf16[4,1024,256]{2,1,0:T(8,128)(2,1)} %bitcast.172), calls=%async_computation.2 | async-start | bytes 4194304 | tf_op jit(solution)/shard_map/all_to_all | solution.py:116
  66.1 7.6 %copy-start.5 = (u32[32]{0:T(128)S(1)}, u32[32]{0:T(128)}, u32[]{:S(2)}) copy-start(u32[32]{0:T(128)} %constant.152) | copy-start | bytes 388
  102.4 38.2 %copy-start.1 = (bf16[1024,256]{1,0:T(8,128)(2,1)S(1)}, bf16[1024,256]{1,0:T(8,128)(2,1)}, u32[]{:S(2)}) copy-start(bf16[1024,256]{1,0:T(8,128)(2,1)} %param.10) | copy-start | bytes 1572868
  105.3 6.6 %collective-permute-start = (bf16[2,256]{1,0:T(2,128)(2,1)S(1)}, bf16[2,256]{1,0:T(2,128)(2,1)S(1)}, u32[]{:S(2)}, u32[]{:S(2)}) collective-permute-start(bf16[2,256]{1,0:T(2,128)(2,1)S(1)} %get-tuple-element.32), channel_id=1, source_target_pairs={{0,2},{2,0},{4,6},{6,4},{8,10},{10,8},{12,14},{14,12},{16,18},{18,... | collective-permute-start | bytes 3080 | tf_op jit(solution)/shard_map/ppermute | solution.py:29
  106.9 9.1 %collective-permute-start.1 = (bf16[2,256]{1,0:T(2,128)(2,1)S(1)}, bf16[2,256]{1,0:T(2,128)(2,1)S(1)}, u32[]{:S(2)}, u32[]{:S(2)}) collective-permute-start(bf16[2,256]{1,0:T(2,128)(2,1)S(1)} %get-tuple-element.31), channel_id=1, source_target_pairs={{0,4},{2,6},{4,0},{6,2},{8,12},{10,14},{12,8},{14,10},{16,20},{18,... | collective-permute-start | bytes 3080 | tf_op jit(solution)/shard_map/ppermute | solution.py:29
  109.2 7.3 %collective-permute-start.2 = (bf16[2,256]{1,0:T(2,128)(2,1)S(1)}, bf16[2,256]{1,0:T(2,128)(2,1)S(1)}, u32[]{:S(2)}, u32[]{:S(2)}) collective-permute-start(bf16[2,256]{1,0:T(2,128)(2,1)S(1)} %get-tuple-element.30), channel_id=1, source_target_pairs={{0,6},{2,4},{4,2},{6,0},{8,14},{10,12},{12,10},{14,8},{16,22},{18,... | collective-permute-start | bytes 3080 | tf_op jit(solution)/shard_map/ppermute | solution.py:29
  109.7 8.4 %collective-permute-start.3 = (bf16[2,256]{1,0:T(2,128)(2,1)S(1)}, bf16[2,256]{1,0:T(2,128)(2,1)S(1)}, u32[]{:S(2)}, u32[]{:S(2)}) collective-permute-start(bf16[2,256]{1,0:T(2,128)(2,1)S(1)} %get-tuple-element.29), channel_id=1, source_target_pairs={{0,8},{2,10},{4,12},{6,14},{8,0},{10,2},{12,4},{14,6},{16,24},{18,... | collective-permute-start | bytes 3080 | tf_op jit(solution)/shard_map/ppermute | solution.py:29
  111.2 7.0 %collective-permute-start.4 = (bf16[2,256]{1,0:T(2,128)(2,1)S(1)}, bf16[2,256]{1,0:T(2,128)(2,1)S(1)}, u32[]{:S(2)}, u32[]{:S(2)}) collective-permute-start(bf16[2,256]{1,0:T(2,128)(2,1)S(1)} %get-tuple-element.28), channel_id=1, source_target_pairs={{0,10},{2,8},{4,14},{6,12},{8,2},{10,0},{12,6},{14,4},{16,26},{18,... | collective-permute-start | bytes 3080 | tf_op jit(solution)/shard_map/ppermute | solution.py:29
  111.8 11.2 %collective-permute-start.5 = (bf16[2,256]{1,0:T(2,128)(2,1)S(1)}, bf16[2,256]{1,0:T(2,128)(2,1)S(1)}, u32[]{:S(2)}, u32[]{:S(2)}) collective-permute-start(bf16[2,256]{1,0:T(2,128)(2,1)S(1)} %get-tuple-element.27), channel_id=1, source_target_pairs={{0,12},{2,14},{4,8},{6,10},{8,4},{10,6},{12,0},{14,2},{16,28},{18,... | collective-permute-start | bytes 3080 | tf_op jit(solution)/shard_map/ppermute | solution.py:29
  116.0 7.6 %collective-permute-start.6 = (bf16[2,256]{1,0:T(2,128)(2,1)S(1)}, bf16[2,256]{1,0:T(2,128)(2,1)S(1)}, u32[]{:S(2)}, u32[]{:S(2)}) collective-permute-start(bf16[2,256]{1,0:T(2,128)(2,1)S(1)} %get-tuple-element.26), channel_id=1, source_target_pairs={{0,14},{2,12},{4,10},{6,8},{8,6},{10,4},{12,2},{14,0},{16,30},{18,... | collective-permute-start | bytes 3080 | tf_op jit(solution)/shard_map/ppermute | solution.py:29
  116.6 8.5 %collective-permute-start.7 = (bf16[2,256]{1,0:T(2,128)(2,1)S(1)}, bf16[2,256]{1,0:T(2,128)(2,1)S(1)}, u32[]{:S(2)}, u32[]{:S(2)}) collective-permute-start(bf16[2,256]{1,0:T(2,128)(2,1)S(1)} %get-tuple-element.25), channel_id=1, source_target_pairs={{0,16},{2,18},{4,20},{6,22},{8,24},{10,26},{12,28},{14,30},{16,0},... | collective-permute-start | bytes 3080 | tf_op jit(solution)/shard_map/ppermute | solution.py:29
  118.1 8.1 %collective-permute-start.8 = (bf16[2,256]{1,0:T(2,128)(2,1)S(1)}, bf16[2,256]{1,0:T(2,128)(2,1)S(1)}, u32[]{:S(2)}, u32[]{:S(2)}) collective-permute-start(bf16[2,256]{1,0:T(2,128)(2,1)S(1)} %get-tuple-element.24), channel_id=1, source_target_pairs={{0,18},{2,16},{4,22},{6,20},{8,26},{10,24},{12,30},{14,28},{16,2},... | collective-permute-start | bytes 3080 | tf_op jit(solution)/shard_map/ppermute | solution.py:29
  118.2 12.7 %collective-permute-start.9 = (bf16[2,256]{1,0:T(2,128)(2,1)S(1)}, bf16[2,256]{1,0:T(2,128)(2,1)S(1)}, u32[]{:S(2)}, u32[]{:S(2)}) collective-permute-start(bf16[2,256]{1,0:T(2,128)(2,1)S(1)} %get-tuple-element.23), channel_id=1, source_target_pairs={{0,20},{2,22},{4,16},{6,18},{8,28},{10,30},{12,24},{14,26},{16,4},... | collective-permute-start | bytes 3080 | tf_op jit(solution)/shard_map/ppermute | solution.py:29
  123.0 9.4 %collective-permute-start.10 = (bf16[2,256]{1,0:T(2,128)(2,1)S(1)}, bf16[2,256]{1,0:T(2,128)(2,1)S(1)}, u32[]{:S(2)}, u32[]{:S(2)}) collective-permute-start(bf16[2,256]{1,0:T(2,128)(2,1)S(1)} %get-tuple-element.22), channel_id=1, source_target_pairs={{0,22},{2,20},{4,18},{6,16},{8,30},{10,28},{12,26},{14,24},{16,6},... | collective-permute-start | bytes 3080 | tf_op jit(solution)/shard_map/ppermute | solution.py:29
  123.6 8.8 %collective-permute-start.11 = (bf16[2,256]{1,0:T(2,128)(2,1)S(1)}, bf16[2,256]{1,0:T(2,128)(2,1)S(1)}, u32[]{:S(2)}, u32[]{:S(2)}) collective-permute-start(bf16[2,256]{1,0:T(2,128)(2,1)S(1)} %get-tuple-element.21), channel_id=1, source_target_pairs={{0,24},{2,26},{4,28},{6,30},{8,16},{10,18},{12,20},{14,22},{16,8},... | collective-permute-start | bytes 3080 | tf_op jit(solution)/shard_map/ppermute | solution.py:29
  125.1 7.3 %collective-permute-start.12 = (bf16[2,256]{1,0:T(2,128)(2,1)S(1)}, bf16[2,256]{1,0:T(2,128)(2,1)S(1)}, u32[]{:S(2)}, u32[]{:S(2)}) collective-permute-start(bf16[2,256]{1,0:T(2,128)(2,1)S(1)} %get-tuple-element.20), channel_id=1, source_target_pairs={{0,26},{2,24},{4,30},{6,28},{8,18},{10,16},{12,22},{14,20},{16,10}... | collective-permute-start | bytes 3080 | tf_op jit(solution)/shard_map/ppermute | solution.py:29
  126.2 6.3 %collective-permute-start.13 = (bf16[2,256]{1,0:T(2,128)(2,1)S(1)}, bf16[2,256]{1,0:T(2,128)(2,1)S(1)}, u32[]{:S(2)}, u32[]{:S(2)}) collective-permute-start(bf16[2,256]{1,0:T(2,128)(2,1)S(1)} %get-tuple-element.19), channel_id=1, source_target_pairs={{0,28},{2,30},{4,24},{6,26},{8,20},{10,22},{12,16},{14,18},{16,12}... | collective-permute-start | bytes 3080 | tf_op jit(solution)/shard_map/ppermute | solution.py:29
  130.9 7.2 %collective-permute-start.14 = (bf16[2,256]{1,0:T(2,128)(2,1)S(1)}, bf16[2,256]{1,0:T(2,128)(2,1)S(1)}, u32[]{:S(2)}, u32[]{:S(2)}) collective-permute-start(bf16[2,256]{1,0:T(2,128)(2,1)S(1)} %get-tuple-element.18), channel_id=1, source_target_pairs={{0,30},{2,28},{4,26},{6,24},{8,22},{10,20},{12,18},{14,16},{16,14}... | collective-permute-start | bytes 3080 | tf_op jit(solution)/shard_map/ppermute | solution.py:29
Sparse Core Ops, SparseCore 0:
  32.0 48.3 all-reduce.2
